TPU v7x, 128 devices: a whole 4x4x4 slice. The times are simulated.
128 devices in a mesh: dp: 32 (over y, x, core), tensor: 4 (over z).
Axes of the slice: x: 4, y: 4, z: 4, core: 2. Of those that a mesh axis runs over, the one named last changes fastest.
Arguments:
- layer_input: bfloat16 [4096, 2560], P('dp'), may hold values from -6 to 6
- inner_out: bfloat16 [4096, 2560], P('dp', 'tensor'), may hold values from -6 to 6
- out_grad: bfloat16 [4096, 2560], P('dp'), may hold values from -0.09375 to 0.09375
- zx_grad: bfloat16 [4096, 5120], P('dp', 'tensor'), may hold values from -0.09375 to 0.09375
- bc_grad: bfloat16 [4096, 1024], P('dp', 'tensor'), may hold values from -0.09375 to 0.09375
- dt_grad: bfloat16 [4096, 40], P('dp', 'tensor'), may hold values from -0.09375 to 0.09375
- owner_deal: int32 [4, 31], P('tensor'), may hold values from 0 to 31, as said below
- head_momentum: float32 [4, 2368, 2560], P('tensor', 'dp'), may hold values from -6 to 6
- bc_momentum: float32 [2, 128, 2560], replicated, may hold values from -6 to 6
Outputs:
- head_update: bfloat16 [40, 3, 64, 2560], P('tensor')
- dt_update: bfloat16 [40, 2560], P('tensor')
- bc_update: bfloat16 [2, 128, 2560], replicated
- head_momentum_out: float32 [4, 2368, 2560], P('tensor', 'dp')
- bc_momentum_out: float32 [2, 128, 2560], replicated
Inputs may be any that keep to these rules, and one draw needn't show every extreme that they name: `owner_deal`: each owner holds at most 1 head blocks of one tensor index; the owner of the dt block (the last entry) holds exactly 1 head blocks of that index as well, so it holds exactly 74 rows.
All inputs are finite; a program needn't handle non-finite values.
Results may differ from a plain program's by a relative error of at most 0.0085.
Values may be sent and summed in bfloat16 or wider, within the bound.
No kernel may reach another device: no remote copies, remote signals or barrier semaphores. Data moves between devices by JAX's collectives and lax.ppermute only.
A program may use at most 128 MiB of HBM per device.

v0:
```python
import math
import jax
import jax.numpy as jnp
from jax import lax
from jax.sharding import PartitionSpec as P

HD = 64
STATE = 128
NS_ITERS = 5
quintic_first = 3.4445
quintic_second = -4.775
quintic_third = 2.0315
momentum_decay = 0.95
norm_epsilon = 1e-07
HEAD_REDUCE = "all_to_all"


def orthogonalize(moment):
    highest = lax.Precision.HIGHEST
    norm_value = jnp.sqrt(jnp.sum(moment * moment, axis=(1, 2), keepdims=True))
    current = moment / (norm_value + norm_epsilon)
    for step in range(NS_ITERS):
        gram_matrix = jnp.einsum("bik,bjk->bij", current, current, precision=highest)
        polynomial = quintic_second * gram_matrix + quintic_third * jnp.einsum(
            "bij,bjk->bik", gram_matrix, gram_matrix, precision=highest
        )
        current = quintic_first * current + jnp.einsum(
            "bij,bjk->bik", polynomial, current, precision=highest
        )
    return current


def on_device(
    layer_input,
    inner_out,
    out_grad,
    zx_grad,
    bc_grad,
    dt_grad,
    owner_deal,
    head_momentum,
    bc_momentum,
):
    n_data = lax.axis_size("dp")
    tokens, width = layer_input.shape
    heads_here = dt_grad.shape[1]
    capacity = head_momentum.shape[1]
    n_blocks = 3 * heads_here
    contract = (((0,), (0,)), ((), ()))
    f32, bf16 = (jnp.float32, jnp.bfloat16)
    owners = owner_deal[0]
    head_owner = owners[:n_blocks]
    dt_owner = owners[n_blocks]
    slots = jnp.arange(n_data, dtype=jnp.int32)
    bc_cols = lax.psum(bc_grad.astype(f32), "tensor")
    bc_part = lax.dot_general(
        bc_cols,
        layer_input.astype(f32),
        contract,
        precision=lax.Precision.HIGHEST,
        preferred_element_type=f32,
    )
    bc_summed = lax.psum(bc_part, "dp")
    zx = zx_grad.reshape(tokens, heads_here, 2, HD)
    io = inner_out.reshape(tokens, heads_here, 1, HD)
    upper = jnp.concatenate([zx, jnp.zeros_like(io)], axis=2).reshape(tokens, n_blocks, HD)
    lower = jnp.concatenate([jnp.zeros_like(zx), io], axis=2).reshape(tokens, n_blocks, HD)
    grad_blocks = jnp.concatenate([upper, lower], axis=0)
    pick = (head_owner[None, :] == slots[:, None]).astype(bf16)
    owner_cols = jnp.einsum("tbr,ob->tor", grad_blocks, pick, preferred_element_type=f32).astype(
        bf16
    )
    dt_cols = jnp.concatenate([dt_grad, jnp.zeros_like(dt_grad)], axis=0)
    is_dt = (slots == dt_owner).astype(bf16)
    dt_owner_cols = dt_cols[:, None, :] * is_dt[None, :, None]
    send_cols = jnp.concatenate([owner_cols, dt_owner_cols], axis=2).reshape(
        2 * tokens, n_data * capacity
    )
    factors = jnp.concatenate([layer_input, out_grad], axis=0)
    send = lax.dot_general(send_cols, factors, contract, preferred_element_type=f32).astype(bf16)
    if HEAD_REDUCE == "all_to_all":
        received = lax.all_to_all(send, "dp", split_axis=0, concat_axis=0, tiled=True)
        owned_sum = jnp.sum(received.reshape(n_data, capacity, width).astype(f32), axis=0)
    else:
        owned_sum = lax.psum_scatter(send, "dp", scatter_dimension=0, tiled=True).astype(f32)
    moment = momentum_decay * head_momentum[0] + owned_sum
    head_direction = orthogonalize(moment[None, :HD])[0]
    dt_direction = orthogonalize(moment[None, HD:])[0]
    owned_update = (
        jnp.concatenate([head_direction, dt_direction], axis=0) * math.sqrt(width)
    ).astype(bf16)
    everything = lax.all_gather(owned_update, "dp", axis=0, tiled=False)
    head_update = jnp.take(everything[:, :HD], head_owner, axis=0, mode="clip").reshape(
        heads_here, 3, HD, width
    )
    dt_update = lax.dynamic_index_in_dim(everything, dt_owner, axis=0, keepdims=False)[HD:]
    bc_moment = momentum_decay * bc_momentum + bc_summed.reshape(2, STATE, width)
    bc_update = (orthogonalize(bc_moment) * math.sqrt(width)).astype(bf16)
    return (head_update, dt_update, bc_update, moment[None], bc_moment)


def solution(mesh):
    in_specs = (
        P("dp", None),
        P("dp", "tensor"),
        P("dp", None),
        P("dp", "tensor"),
        P("dp", "tensor"),
        P("dp", "tensor"),
        P("tensor", None),
        P("tensor", "dp", None),
        P(),
    )
    out_specs = (
        P("tensor", None, None, None),
        P("tensor", None),
        P(),
        P("tensor", "dp", None),
        P(),
    )
    return jax.shard_map(
        on_device, mesh=mesh, in_specs=in_specs, out_specs=out_specs, check_vma=False
    )
```

profile of v0, /device:TPU:1, one launch (start us, length us, event | category | flops | bytes accessed | tf_op | source)
XLA Modules:
  0.0 375.3 jit_solution(5837344694989984997)
XLA Ops:
  7.2 1.2 slice.24
  8.4 0.7 slice_bitcast_fusion
  9.1 0.6 compare_convert_fusion
  9.7 1.1 copy.28
  10.8 0.7 concatenate.35
  11.6 0.3 copy.31
  11.9 1.2 copy.27
  13.2 0.3 copy.30
  13.6 0.4 fusion.4
  14.1 0.7 copy.32
  14.8 0.4 reshape.316
  15.2 7.2 %convolution_convert_fusion = bf16[2368,2560]{1,0:T(8,128)(2,1)} fusion(bf16[256,2368]{0,1:T(8,128)(2,1)S(1)} %reshape.316, bf16[128,2560]{1,0:T(8,128)(2,1)} %param.11, bf16[128,2560]{1,0:T(8,128)(2,1)S(1)} %copy-done.1), kind=kOutput, calls=%fused_computation.2 | convolution fusion | flops 3112468480 | bytes 14647296 | tf_op jit(solution)/shard_map/dot_general | solution.py:80
  22.4 12.3 %all_to_all.6 = bf16[32,74,2560]{2,1,0:T(8,128)(2,1)} reshape(bf16[2368,2560]{1,0:T(8,128)(2,1)} %convolution_convert_fusion) | data formatting | bytes 24248320 | tf_op jit(solution)/shard_map/all_to_all | solution.py:82
  34.7 8.8 %all-to-all-start = ((bf16[32,74,2560]{2,1,0:T(8,128)(2,1)}), bf16[32,74,2560]{2,1,0:T(8,128)(2,1)}, u32[]{:S(2)}, u32[]{:S(2)}) async-start(bf16[32,74,2560]{2,1,0:T(8,128)(2,1)} %all_to_all.6), calls=%async_computation | async-start | bytes 26214400 | tf_op jit(solution)/shard_map/all_to_all | solution.py:82
  43.5 17.5 %all-reduce.7 = f32[128,256]{1,0:T(8,128)S(1)} all-reduce(bf16[128,256]{1,0:T(8,128)(2,1)S(1)} %copy-done.3), channel_id=1, replica_groups=mesh['dp'=32,'tensor'=4] {'tensor'}, use_global_device_ids=true, to_apply=%region_3.0 | all-reduce | flops 32768 | bytes 196608 | tf_op jit(solution)/shard_map/psum | solution.py:55
  61.0 2.7 fusion.43
  63.8 0.6 all-gather.2.cloned.1.call-start
  64.3 139.2 %all-to-all-done = bf16[32,74,2560]{2,1,0:T(8,128)(2,1)} async-done(((bf16[32,74,2560]{2,1,0:T(8,128)(2,1)}), bf16[32,74,2560]{2,1,0:T(8,128)(2,1)}, u32[]{:S(2)}, u32[]{:S(2)}) %all-to-all-start) | async-done | bytes 12124192 | tf_op jit(solution)/shard_map/all_to_all | solution.py:82
  203.6 6.8 %convert_reduce_fusion = f32[74,2560]{1,0:T(8,128)S(1)} fusion(bf16[32,74,2560]{2,1,0:T(8,128)(2,1)} %all-to-all-done), kind=kLoop, calls=%fused_computation.1 | loop fusion | flops 11934720 | bytes 12881920 | tf_op jit(solution)/shard_map/reduce_sum | solution.py:83
  210.6 0.6 multiply_reduce_fusion.2
  211.2 0.8 multiply_reduce_fusion.1
  213.4 0.3 fusion.29
  213.8 0.7 fusion.28
  214.7 0.3 convolution_add_fusion.14
  215.0 0.7 convolution_add_fusion.9
  215.7 0.3 fusion.39
  216.2 0.3 convolution_add_fusion.13
  216.5 0.3 fusion.40
  216.9 0.3 convolution_add_fusion.12
  217.2 0.3 fusion.41
  217.7 0.3 convolution_add_fusion.11
  218.0 0.3 fusion.42
  218.5 0.7 fusion.35
  219.3 0.7 convolution_add_fusion.8
  220.0 0.7 fusion.36
  220.9 0.7 convolution_add_fusion.7
  221.6 0.7 fusion.37
  222.4 0.3 fusion.3
  222.7 0.7 convolution_add_fusion.6
  223.4 0.7 fusion.38
  224.2 0.7 fusion.2
  224.9 0.8 fusion.26
  227.7 53.1 %all-reduce.6.cloned.1.call-done = f32[2,128,2560]{2,1,0:T(8,128)} async-done(((f32[2,128,2560]{2,1,0:T(8,128)}), f32[2,128,2560]{2,1,0:T(8,128)}) %all-reduce.6.cloned.1.call-update) | async-done | bytes 2621456 | tf_op jit(solution)/shard_map/psum | solution.py:63
  280.9 3.2 multiply_reduce_fusion
  284.0 2.9 fusion.27
  287.0 0.3 fusion.12
  287.3 2.7 convolution_add_fusion.4
  289.9 2.5 fusion.44
  292.4 0.3 fusion.11
  292.7 2.6 convolution_add_fusion.3
  295.4 2.7 fusion.45
  298.1 0.3 fusion.10
  298.4 2.6 convolution_add_fusion.2
  301.0 2.5 fusion.46
  303.5 0.3 fusion.9
  303.8 2.6 convolution_add_fusion.1
  306.5 2.5 fusion.47
  309.0 0.3 fusion.8
  309.3 4.0 %fusion.1 = bf16[2,128,2560]{2,1,0:T(8,128)(2,1)} fusion(f32[2,128,128]{2,1,0:T(8,128)S(1)} %fusion.8, f32[2,128,2560]{2,1,0:T(8,128)S(1)} %convolution_add_fusion.1), kind=kOutput, calls=%fused_computation.9 | convolution fusion | flops 1009254400 | bytes 4063232 | tf_op jit(solution)/shard_map/bij,bjk->bik/dot_general | solution.py:27
  313.4 1.6 copy.33
  315.0 32.9 %all-gather.2.cloned.1.call-done = bf16[32,74,2560]{2,1,0:T(8,128)(2,1)} async-done(((bf16[1,74,2560]{2,1,0:T(8,128)(2,1)}), bf16[32,74,2560]{2,1,0:T(8,128)(2,1)}) %all-gather.2.cloned.1.call-update) | async-done | bytes 12124176 | tf_op jit(solution)/shard_map/all_gather | solution.py:92
  347.9 9.0 %slice.34 = bf16[32,64,2560]{2,1,0:T(8,128)(2,1)} slice(bf16[32,74,2560]{2,1,0:T(8,128)(2,1)} %all-gather.2.cloned.1.call-done), slice={[0:32], [0:64], [0:2560]} | slice | bytes 20971520 | tf_op jit(solution)/shard_map/slice | solution.py:93
  356.8 9.9 %gather_fusion = bf16[30,64,2560]{2,1,0:T(8,128)(2,1)} fusion(bf16[32,64,2560]{2,1,0:T(8,128)(2,1)} %slice.34, s32[1024]{0:T(1024)S(1)} %pad_clamp_fusion), kind=kCustom, calls=%fused_computation | custom fusion | bytes 19660920 | tf_op jit(solution)/shard_map/jit(_take)/gather | solution.py:93
  366.7 1.5 dynamic-slice_bitcast_fusion
  (29 shorter events, 2.4 us)
Async XLA Ops:
  14.1 1.1 copy-start.1
  34.7 8.8 %copy-start.3 = (bf16[128,256]{1,0:T(8,128)(2,1)S(1)}, bf16[128,256]{1,0:T(8,128)(2,1)}, u32[]{:S(2)}) copy-start(bf16[128,256]{1,0:T(8,128)(2,1)} %param.13) | copy-start | bytes 196612
  34.7 168.9 %all-to-all-start = ((bf16[32,74,2560]{2,1,0:T(8,128)(2,1)}), bf16[32,74,2560]{2,1,0:T(8,128)(2,1)}, u32[]{:S(2)}, u32[]{:S(2)}) async-start(bf16[32,74,2560]{2,1,0:T(8,128)(2,1)} %all_to_all.6), calls=%async_computation | async-start | bytes 26214400 | tf_op jit(solution)/shard_map/all_to_all | solution.py:82
  43.5 237.4 %all-reduce.6.cloned.1.call-start = ((), (), s32[]{:S(2)}) async-start(), calls=%async_computation.2 | async-start | bytes 5242880 | tf_op jit(solution)/shard_map/psum | solution.py:63
  63.8 146.7 %copy-start = (f32[1,74,2560]{2,0,1:T(1,128)S(1)}, f32[1,74,2560]{2,0,1:T(1,128)}, u32[]{:S(2)}) copy-start(f32[1,74,2560]{2,0,1:T(1,128)} %param.16) | copy-start | bytes 2273284
  63.8 284.1 %all-gather.2.cloned.1.call-start = ((), (), s32[]{:S(2)}) async-start(), calls=%async_computation.1 | async-start | bytes 13516800 | tf_op jit(solution)/shard_map/all_gather | solution.py:92
  284.0 3.2 copy-start.2
Sparse Core Ops, SparseCore 0:
  63.9 216.9 all-reduce.5
  283.7 64.1 all-gather.1
where the time goes:
time: 381 us; the launch traced here: 375 us
  waiting for transfers between devices  225 us (59%)
  matrix products  50.9 us (13%)
  local copies, waits for them, and re-layouts  41 us (11%)
  between operations  18 us (5%)
  blocking collectives  17.5 us (5%)
  other arithmetic  13.3 us (3%)
  starting transfers between devices  9.36 us (2%)
    all_to_all x1, waiting for transfers between devices, on_device(): lax.all_to_all(send, 'dp', split_axis=0, concat_axis=0, tiled=True)  139 us
    psum x1, waiting for transfers between devices, on_device(): bc_summed = lax.psum(bc_part, 'dp')  53.1 us
    all_gather x1, waiting for transfers between devices, on_device(): everything = lax.all_gather(owned_update, 'dp', axis=0, tiled=False)  32.9 us
    dot_general x15, matrix products, orthogonalize(): jnp.einsum('bij,bjk->bik', polynomial, current, precision=highest)  19.5 us
    dot_general x15, matrix products, orthogonalize(): jnp.einsum('bik,bjk->bij', current, current, precision=highest)  18 us
    psum x1, blocking collectives, on_device(): bc_cols = lax.psum(bc_grad.astype(f32), 'tensor')  17.5 us
    all_to_all x1, local copies, waits for them, and re-layouts, on_device(): lax.all_to_all(send, 'dp', split_axis=0, concat_axis=0, tiled=True)  12.3 us
    gather x1, local copies, waits for them, and re-layouts, on_device(): jnp.take(everything[:, :HD], head_owner, axis=0, mode='clip')  9.86 us
  transfers between devices with their start and end apart: 3, of which 3 were waited for; matrix products, arithmetic and copies ran while one was open for 15% of the time, Pallas kernels for 0%

commit v1 on v0

--- a/solution.py
+++ b/solution.py
@@ -60,7 +60,11 @@
         precision=lax.Precision.HIGHEST,
         preferred_element_type=f32,
     )
-    bc_summed = lax.psum(bc_part, "dp")
+    bc_summed = bc_part
+    for hop in (1, 2, 4, 8, 16):
+        bc_summed = bc_summed + lax.ppermute(
+            bc_summed, "dp", [(dev, dev ^ hop) for dev in range(32)]
+        )
     zx = zx_grad.reshape(tokens, heads_here, 2, HD)
     io = inner_out.reshape(tokens, heads_here, 1, HD)
     upper = jnp.concatenate([zx, jnp.zeros_like(io)], axis=2).reshape(tokens, n_blocks, HD)

time: 381 us -> 564 us (1.48)
  blocking collectives: 17.5 us -> 172 us
  waiting for transfers between devices: 225 us -> 254 us
    ppermute x0 -> x5, waiting for transfers between devices: none -> 254 us  [on_device(): lax.ppermute(bc_summed, 'dp', [(dev, dev ^ hop) for dev in range(32)])]
    all_to_all x0 -> x1, blocking collectives: none -> 155 us  [on_device(): lax.all_to_all(send, 'dp', split_axis=0, concat_axis=0, tiled=True)]
    all_to_all x1 -> x0, waiting for transfers between devices: 139 us -> none  [on_device(): lax.all_to_all(send, 'dp', split_axis=0, concat_axis=0, tiled=True)]
    psum x1 -> x0, waiting for transfers between devices: 53.1 us -> none  [on_device(): bc_summed = lax.psum(bc_part, 'dp')]
    all_gather x1, waiting for transfers between devices: 32.9 us -> 0.01 us  [on_device(): everything = lax.all_gather(owned_update, 'dp', axis=0, tiled=False)]
    all_to_all x1 -> x0, starting transfers between devices: 8.75 us -> none  [on_device(): lax.all_to_all(send, 'dp', split_axis=0, concat_axis=0, tiled=True)]
    ppermute x0 -> x5, starting transfers between devices: none -> 6.75 us  [on_device(): lax.ppermute(bc_summed, 'dp', [(dev, dev ^ hop) for dev in range(32)])]
  transfers between devices with their start and end apart: 3 -> 6, of which waited for: 3 -> 5; matrix products, arithmetic and copies ran while one was open for 15% -> 7% of each run, Pallas kernels for 0% -> 0%
where the time goes in v1:
time: 564 us; the launch traced here: 557 us
  waiting for transfers between devices  254 us (45%)
  blocking collectives  172 us (30%)
  matrix products  49.9 us (9%)
  local copies, waits for them, and re-layouts  41.1 us (7%)
  between operations  18.3 us (3%)
  other arithmetic  15.3 us (3%)
  starting transfers between devices  6.79 us (1%)
    ppermute x5, waiting for transfers between devices, on_device(): lax.ppermute(bc_summed, 'dp', [(dev, dev ^ hop) for dev in range(32)])  254 us
    all_to_all x1, blocking collectives, on_device(): lax.all_to_all(send, 'dp', split_axis=0, concat_axis=0, tiled=True)  155 us
    dot_general x15, matrix products, orthogonalize(): jnp.einsum('bij,bjk->bik', polynomial, current, precision=highest)  19.5 us
    dot_general x15, matrix products, orthogonalize(): jnp.einsum('bik,bjk->bij', current, current, precision=highest)  18.4 us
    psum x1, blocking collectives, on_device(): bc_cols = lax.psum(bc_grad.astype(f32), 'tensor')  16.1 us
    all_to_all x1, local copies, waits for them, and re-layouts, on_device(): lax.all_to_all(send, 'dp', split_axis=0, concat_axis=0, tiled=True)  12.3 us
  transfers between devices with their start and end apart: 6, of which 5 were waited for; matrix products, arithmetic and copies ran while one was open for 7% of the time, Pallas kernels for 0%

profile of v1, /device:TPU:1, one launch (start us, length us, event | category | flops | bytes accessed | tf_op | source)
XLA Modules:
  0.0 556.9 jit_solution(14770461843253979926)
XLA Ops:
  7.2 1.2 slice.24
  8.4 0.7 slice_bitcast_fusion
  9.1 0.6 compare_convert_fusion
  9.8 1.1 copy.28
  10.8 0.7 concatenate.35
  11.6 0.3 copy.31
  12.0 1.2 copy.27
  13.2 0.3 copy.30
  13.6 0.4 fusion.4
  14.2 0.7 copy.32
  14.9 0.4 reshape.316
  15.3 7.2 %convolution_convert_fusion = bf16[2368,2560]{1,0:T(8,128)(2,1)} fusion(bf16[256,2368]{0,1:T(8,128)(2,1)S(1)} %reshape.316, bf16[128,2560]{1,0:T(8,128)(2,1)} %param.11, bf16[128,2560]{1,0:T(8,128)(2,1)S(1)} %copy-done.1), kind=kOutput, calls=%fused_computation.2 | convolution fusion | flops 3112468480 | bytes 14647296 | tf_op jit(solution)/shard_map/dot_general | solution.py:84
  22.4 12.3 %all_to_all.6 = bf16[32,74,2560]{2,1,0:T(8,128)(2,1)} reshape(bf16[2368,2560]{1,0:T(8,128)(2,1)} %convolution_convert_fusion) | data formatting | bytes 24248320 | tf_op jit(solution)/shard_map/all_to_all | solution.py:86
  34.8 155.5 %all_to_all.9 = bf16[32,74,2560]{2,1,0:T(8,128)(2,1)} all-to-all(bf16[32,74,2560]{2,1,0:T(8,128)(2,1)} %all_to_all.6), channel_id=1, replica_groups=mesh['dp'=32,'tensor'=4] {'dp'}, dimensions={0} | all-to-all | bytes 24248320 | tf_op jit(solution)/shard_map/all_to_all | solution.py:86
  190.3 6.9 %convert_reduce_fusion = f32[74,2560]{1,0:T(8,128)S(1)} fusion(bf16[32,74,2560]{2,1,0:T(8,128)(2,1)} %all_to_all.9), kind=kLoop, calls=%fused_computation.1 | loop fusion | flops 11934720 | bytes 12881920 | tf_op jit(solution)/shard_map/reduce_sum | solution.py:87
  197.3 0.6 multiply_reduce_fusion.2
  197.9 0.8 multiply_reduce_fusion.1
  200.1 0.3 fusion.29
  200.6 0.7 fusion.28
  201.7 0.7 convolution_add_fusion.8
  202.9 0.3 convolution_add_fusion.12
  204.4 0.3 convolution_add_fusion.10
  205.2 0.3 fusion.3
  205.5 0.7 fusion.39
  206.3 0.7 convolution_add_fusion.7
  207.0 0.7 fusion.40
  207.9 0.7 convolution_add_fusion.6
  208.6 0.7 fusion.41
  209.4 0.7 convolution_add_fusion.5
  210.1 0.7 fusion.42
  211.0 0.7 fusion.2
  211.7 0.8 fusion.27
  212.5 16.1 %all-reduce.4 = f32[128,256]{1,0:T(8,128)S(1)} all-reduce(bf16[128,256]{1,0:T(8,128)(2,1)S(1)} %copy-done.5), channel_id=1, replica_groups=mesh['dp'=32,'tensor'=4] {'tensor'}, use_global_device_ids=true, to_apply=%region_3.0 | all-reduce | flops 32768 | bytes 196608 | tf_op jit(solution)/shard_map/psum | solution.py:55
  228.6 1.2 fusion.47
  229.8 4.2 collective-permute-start
  234.1 4.5 collective-permute-done
  238.6 0.3 add.186
  238.9 0.4 collective-permute-start.1
  239.3 84.1 %collective-permute-done.1 = f32[256,2560]{1,0:T(8,128)S(1)} collective-permute-done((f32[256,2560]{1,0:T(8,128)S(1)}, f32[256,2560]{1,0:T(8,128)S(1)}, u32[]{:S(2)}, u32[]{:S(2)}) %collective-permute-start.1) | collective-permute-done | bytes 2621472 | tf_op jit(solution)/shard_map/ppermute | solution.py:65
  323.4 0.3 add.187
  323.7 1.2 collective-permute-start.2
  324.9 57.6 %collective-permute-done.2 = f32[256,2560]{1,0:T(8,128)S(1)} collective-permute-done((f32[256,2560]{1,0:T(8,128)S(1)}, f32[256,2560]{1,0:T(8,128)S(1)}, u32[]{:S(2)}, u32[]{:S(2)}) %collective-permute-start.2) | collective-permute-done | bytes 2621472 | tf_op jit(solution)/shard_map/ppermute | solution.py:65
  382.5 0.3 add.188
  382.9 56.3 %collective-permute-done.3 = f32[256,2560]{1,0:T(8,128)S(1)} collective-permute-done((f32[256,2560]{1,0:T(8,128)S(1)}, f32[256,2560]{1,0:T(8,128)S(1)}, u32[]{:S(2)}, u32[]{:S(2)}) %collective-permute-start.3) | collective-permute-done | bytes 2621472 | tf_op jit(solution)/shard_map/ppermute | solution.py:65
  439.2 0.3 add.189
  439.5 0.9 collective-permute-start.4
  442.4 1.2 bitcast_add_fusion
  443.7 1.6 copy.33
  445.3 51.4 %collective-permute-done.4 = f32[256,2560]{1,0:T(8,128)} collective-permute-done((f32[256,2560]{1,0:T(8,128)S(1)}, f32[256,2560]{1,0:T(8,128)}, u32[]{:S(2)}, u32[]{:S(2)}) %collective-permute-start.4) | collective-permute-done | bytes 2621472 | tf_op jit(solution)/shard_map/ppermute | solution.py:65
  496.7 2.0 add.190
  498.8 0.7 multiply_reduce_fusion
  499.5 2.8 fusion.38
  502.5 2.4 fusion.37
  505.0 3.1 fusion.26
  508.4 3.3 convolution_add_fusion.3
  511.6 2.5 fusion.48
  514.4 2.6 convolution_add_fusion.2
  517.0 2.5 fusion.49
  519.8 2.6 convolution_add_fusion.1
  522.5 2.8 fusion.50
  525.5 3.7 fusion.1
  529.3 9.0 %slice.34 = bf16[32,64,2560]{2,1,0:T(8,128)(2,1)} slice(bf16[32,74,2560]{2,1,0:T(8,128)(2,1)} %all-gather.2.cloned.1.call-done), slice={[0:32], [0:64], [0:2560]} | slice | bytes 20971520 | tf_op jit(solution)/shard_map/slice | solution.py:97
  538.2 9.9 %gather_fusion = bf16[30,64,2560]{2,1,0:T(8,128)(2,1)} fusion(bf16[32,64,2560]{2,1,0:T(8,128)(2,1)} %slice.34, s32[1024]{0:T(1024)S(1)} %pad_clamp_fusion), kind=kCustom, calls=%fused_computation | custom fusion | bytes 19660920 | tf_op jit(solution)/shard_map/jit(_take)/gather | solution.py:97
  548.1 1.5 dynamic-slice_bitcast_fusion
  (44 shorter events, 5.4 us)
Async XLA Ops:
  7.2 522.1 %all-gather.2.cloned.1.call-start = ((), (), s32[]{:S(2)}) async-start(), calls=%async_computation.1 | async-start | bytes 13516800 | tf_op jit(solution)/shard_map/all_gather | solution.py:96
  14.2 1.1 copy-start.1
  190.2 6.9 %copy-start = (f32[1,74,2560]{2,0,1:T(1,128)S(1)}, f32[1,74,2560]{2,0,1:T(1,128)}, u32[]{:S(2)}) copy-start(f32[1,74,2560]{2,0,1:T(1,128)} %param.16) | copy-start | bytes 2273284
  209.4 3.1 copy-start.5
  210.1 18.5 %copy-start.2 = (bf16[128,2560]{1,0:T(8,128)(2,1)S(1)}, bf16[128,2560]{1,0:T(8,128)(2,1)}, u32[]{:S(2)}) copy-start(bf16[128,2560]{1,0:T(8,128)(2,1)} %param.9) | copy-start | bytes 1966084
  229.8 8.8 %collective-permute-start = (f32[256,2560]{1,0:T(8,128)S(1)}, f32[256,2560]{1,0:T(8,128)S(1)}, u32[]{:S(2)}, u32[]{:S(2)}) collective-permute-start(f32[256,2560]{1,0:T(8,128)S(1)} %fusion.47), channel_id=1, source_target_pairs={{0,4},{4,0},{8,12},{12,8},{16,20},{20,16},{24,28},{28,24},{32,36},... | collective-permute-start | bytes 7864328 | tf_op jit(solution)/shard_map/ppermute | solution.py:65
  238.9 84.5 %collective-permute-start.1 = (f32[256,2560]{1,0:T(8,128)S(1)}, f32[256,2560]{1,0:T(8,128)S(1)}, u32[]{:S(2)}, u32[]{:S(2)}) collective-permute-start(f32[256,2560]{1,0:T(8,128)S(1)} %add.186), channel_id=1, source_target_pairs={{0,8},{4,12},{8,0},{12,4},{16,24},{20,28},{24,16},{28,20},{32,40},... | collective-permute-start | bytes 7864328 | tf_op jit(solution)/shard_map/ppermute | solution.py:65
  323.7 58.8 %collective-permute-start.2 = (f32[256,2560]{1,0:T(8,128)S(1)}, f32[256,2560]{1,0:T(8,128)S(1)}, u32[]{:S(2)}, u32[]{:S(2)}) collective-permute-start(f32[256,2560]{1,0:T(8,128)S(1)} %add.187), channel_id=1, source_target_pairs={{0,16},{4,20},{8,24},{12,28},{16,0},{20,4},{24,8},{28,12},{32,48},... | collective-permute-start | bytes 7864328 | tf_op jit(solution)/shard_map/ppermute | solution.py:65
  382.8 56.4 %collective-permute-start.3 = (f32[256,2560]{1,0:T(8,128)S(1)}, f32[256,2560]{1,0:T(8,128)S(1)}, u32[]{:S(2)}, u32[]{:S(2)}) collective-permute-start(f32[256,2560]{1,0:T(8,128)S(1)} %add.188), channel_id=1, source_target_pairs={{0,32},{4,36},{8,40},{12,44},{16,48},{20,52},{24,56},{28,60},{32,0... | collective-permute-start | bytes 7864328 | tf_op jit(solution)/shard_map/ppermute | solution.py:65
  439.5 57.2 %collective-permute-start.4 = (f32[256,2560]{1,0:T(8,128)S(1)}, f32[256,2560]{1,0:T(8,128)}, u32[]{:S(2)}, u32[]{:S(2)}) collective-permute-start(f32[256,2560]{1,0:T(8,128)S(1)} %add.189), channel_id=1, source_target_pairs={{0,64},{4,68},{8,72},{12,76},{16,80},{20,84},{24,88},{28,92},{32,9... | collective-permute-start | bytes 7864328 | tf_op jit(solution)/shard_map/ppermute | solution.py:65
  445.3 53.4 %copy-start.3 = (f32[2,128,2560]{2,1,0:T(8,128)S(1)}, f32[2,128,2560]{2,1,0:T(8,128)}, u32[]{:S(2)}) copy-start(f32[2,128,2560]{2,1,0:T(8,128)} %param.17) | copy-start | bytes 7864324
  499.5 8.9 %copy-start.4 = (f32[2,128,2560]{2,1,0:T(8,128)}, f32[2,128,2560]{2,1,0:T(8,128)S(1)}, u32[]{:S(2)}) copy-start(f32[2,128,2560]{2,1,0:T(8,128)S(1)} %get-tuple-element.21) | copy-start | bytes 7864324
Sparse Core Ops, SparseCore 0:
  212.6 87.8 all-gather.1
